TPU v7x, 256 devices: a whole 4x4x8 slice. The times are simulated.
256 devices in a mesh: person: 2 (over x_lo), tm: 32 (over y, z), mp: 4 (over x_hi, core).
Axes of the slice: x: 4 (x_hi: 2, x_lo: 2; x = x_hi * 2 + x_lo), y: 4, z: 8, core: 2. Of those that a mesh axis runs over, the one named last changes fastest.
Arguments:
- motion: bfloat16 [2, 2, 8192, 2048], P('person', None, 'tm', 'mp'), may hold values from -6 to 6
- valid: int32 [2, 2, 8192], P('person', None, 'tm'), may hold values from 0 to 1, as said below
- windows: int32 [32], replicated, may hold values from 64 to 512, as said below
- gains: float32 [2, 2048], replicated, may hold values from 0.5 to 1.5
- w_self_in: bfloat16 [2048, 3072], P('tm', 'mp')
- w_self_out: bfloat16 [2048, 2048], P('mp', 'tm'), may hold values from -0.125 to 0.125
- w_cross_in: bfloat16 [2048, 3072], P('tm', 'mp')
- w_cross_out: bfloat16 [2048, 2048], P('mp', 'tm'), may hold values from -0.125 to 0.125
Outputs:
- mixed: bfloat16 [2, 2, 8192, 2048], P('person', None, 'tm', 'mp')
Inputs may be any that keep to these rules, and one draw needn't show every extreme that they name: `valid`: for each person and clip the frames with 1 form a prefix that covers at least half of the 8192 frames and never all of them. `windows`: some head's window is exactly 512.
All inputs are finite; a program needn't handle non-finite values.
Results may differ from a plain program's by a relative error of at most 0.035.
The roundings to bfloat16 on the way count: a program that leaves them out, or rounds other values in their place, can miss the bound.
Values may be sent and summed in bfloat16 or wider, within the bound.
No kernel may reach another device: no remote copies, remote signals or barrier semaphores. Data moves between devices by JAX's collectives and lax.ppermute only.
A program may use at most 64 MiB of HBM per device.

v0:
```python
import jax
import jax.numpy as jnp
from jax import lax
from jax.sharding import PartitionSpec as P

D = 2048
HEADS = 32
KV_HEADS = 8
HEAD_DIM = 64
WIN = 512
EPS = 1e-05


def passed_along(value, axis, steps):
    count = lax.axis_size(axis)
    leading, last = (max(0, -steps), min(count, count - steps))
    return lax.ppermute(value, axis, [(source, source + steps) for source in range(leading, last)])


def swapped(value, axis, apart):
    mask = 2**apart
    pairs = [(source, source ^ mask) for source in range(lax.axis_size(axis))]
    return lax.ppermute(value, axis, pairs)


def rms_normed(rows, gain):
    values = rows.astype(jnp.float32)
    scale = lax.rsqrt(jnp.mean(values * values, axis=-1, keepdims=True) + EPS)
    return (values * scale * gain).astype(jnp.bfloat16)


def project_in(normed_rows, weight_rows):
    total = jnp.dot(
        normed_rows,
        lax.all_gather(weight_rows, "tm", axis=0, tiled=True),
        preferred_element_type=jnp.float32,
    )
    return total.astype(jnp.bfloat16)


def earlier_frames(pair, frames):
    pieces = [pair]
    for step in range(1, WIN // frames + 1):
        pieces.insert(0, passed_along((pair[0], pair[1]), "tm", step))
    key_vals = jnp.concatenate([piece[0] for piece in pieces], 1)
    masks = jnp.concatenate([piece[1] for piece in pieces], 1)
    return (key_vals, masks)


def window_attend(queries, key_vals, masks, wins):
    count_q = queries.shape[1]
    count_k = key_vals.shape[1]
    dist = jnp.arange(count_q)[:, None] + (count_k - count_q) - jnp.arange(count_k)[None, :]

    def one_clip(items):
        query, pairs, kvalid = items
        keys = pairs[:, :, 0]
        values = pairs[:, :, 1]
        allowed = (
            (dist >= 0)
            & (dist < wins[:, :, None, None])
            & ((kvalid[None, None, None, :] == 1) | (dist == 0))
        )
        scores = jnp.einsum(
            "qkgd,ckd->kgqc", query, keys, preferred_element_type=jnp.float32
        ) * HEAD_DIM ** (-0.5)
        top = jnp.max(jnp.where(allowed, scores, -1e30), axis=-1, keepdims=True)
        exps = jnp.where(allowed, jnp.exp(scores - top), 0.0)
        total = jnp.sum(exps, axis=-1)
        weights = exps.astype(jnp.bfloat16)
        summed = jnp.einsum("kgqc,ckd->qkgd", weights, values, preferred_element_type=jnp.float32)
        return (summed / jnp.transpose(total, (2, 0, 1))[..., None]).astype(jnp.bfloat16)

    outputs = lax.map(one_clip, (queries, key_vals, masks))
    return outputs.reshape(outputs.shape[0] * outputs.shape[1], -1)


def project_out(heads, weight, residual):
    terms = jnp.dot(
        heads, lax.all_gather(weight, "tm", axis=1, tiled=True), preferred_element_type=jnp.float32
    )
    summed = lax.psum_scatter(terms, "mp", scatter_dimension=1, tiled=True)
    return (residual.astype(jnp.float32) + summed).astype(jnp.bfloat16)


def body(motion, valid, windows, gains, w_self_in, w_self_out, w_cross_in, w_cross_out):
    clips = motion.shape[1]
    frames = motion.shape[2]
    count = clips * frames
    group = HEADS // KV_HEADS
    local_heads = w_self_out.shape[0] // HEAD_DIM
    local_groups = local_heads // group
    wins = lax.dynamic_slice_in_dim(
        windows, lax.axis_index("mp") * local_heads, local_heads, 0
    ).reshape(local_groups, group)
    own_valid = valid[0]
    residual = motion.reshape(count, motion.shape[3])
    full = lax.all_gather(motion, "mp", axis=3, tiled=True).reshape(count, D)
    normed = rms_normed(full, gains[0])
    self_proj = project_in(normed, w_self_in).reshape(
        clips, frames, local_groups, group + 2, HEAD_DIM
    )
    self_pair = self_proj[:, :, :, group:]
    key_vals, masks = earlier_frames((self_pair, own_valid), frames)
    self_heads = window_attend(self_proj[:, :, :, :group], key_vals, masks, wins)
    hidden = project_out(self_heads, w_self_out, residual)
    hidden_full = lax.all_gather(hidden, "mp", axis=1, tiled=True)
    normed2 = rms_normed(hidden_full, gains[1])
    cross_proj = project_in(normed2, w_cross_in).reshape(
        clips, frames, local_groups, group + 2, HEAD_DIM
    )
    cross_pair = cross_proj[:, :, :, group:]
    partner = swapped((cross_pair, own_valid), "person", 0)
    partner_vals, partner_masks = earlier_frames(partner, frames)
    cross_heads = window_attend(cross_proj[:, :, :, :group], partner_vals, partner_masks, wins)
    mixed = project_out(cross_heads, w_cross_out, hidden)
    return mixed.reshape(motion.shape)


def solution(mesh):
    in_specs = (
        P("person", None, "tm", "mp"),
        P("person", None, "tm"),
        P(),
        P(),
        P("tm", "mp"),
        P("mp", "tm"),
        P("tm", "mp"),
        P("mp", "tm"),
    )
    out_specs = P("person", None, "tm", "mp")
    return jax.shard_map(body, mesh=mesh, in_specs=in_specs, out_specs=out_specs, check_vma=False)
```

profile of v0, /device:TPU:1, one launch (start us, length us, event | category | flops | bytes accessed | tf_op | source)
XLA Modules:
  0.0 520.7 jit_solution(5809093448599657538)
XLA Ops:
  6.5 0.7 all-gather.7.cloned.1.call-update
  7.3 0.7 all-gather.9.cloned.1.call-update
  8.1 0.7 all-gather.11.cloned.1.call-update
  8.8 0.8 fusion.121
  9.6 32.9 %all-gather.7.cloned.1.call-done = bf16[1,2,256,2048]{3,2,1,0:T(8,128)(2,1)} async-done(((bf16[1,2,256,512]{3,2,1,0:T(8,128)(2,1)}), bf16[1,2,256,2048]{3,2,1,0:T(8,128)(2,1)}) %all-gather.7.cloned.1.call-update) | async-done | bytes 2097168 | tf_op jit(solution)/shard_map/all_gather | solution.py:98
  42.5 2.2 multiply_reduce_fusion
  44.8 0.5 fusion.102
  45.3 74.5 %all-gather.9.cloned.1.call-done = bf16[2048,768]{1,0:T(8,128)(2,1)} async-done(((bf16[64,768]{1,0:T(8,128)(2,1)}), bf16[2048,768]{1,0:T(8,128)(2,1)}) %all-gather.9.cloned.1.call-update) | async-done | bytes 3145744 | tf_op jit(solution)/shard_map/all_gather | solution.py:35
  119.8 3.7 convolution_convert_fusion
  124.1 3.5 collective-permute-start
  127.6 3.1 collective-permute-start.1
  130.8 3.1 collective-permute-start.2
  133.9 2.4 collective-permute-start.3
  136.4 5.5 %collective-permute-done.2 = s32[2,256]{1,0:T(2,128)S(1)} collective-permute-done((s32[2,256]{1,0:T(2,128)S(1)}, s32[2,256]{1,0:T(2,128)S(1)}, u32[]{:S(2)}, u32[]{:S(2)}) %collective-permute-start.2) | collective-permute-done | bytes 2080 | tf_op jit(solution)/shard_map/ppermute | solution.py:17
  142.4 0.8 pad_maximum_fusion
  143.4 19.0 %while.24 = (s32[]{:T(128)}, bf16[2,256,2,4,64]{1,4,3,2,0:T(8,128)(2,1)S(1)}, bf16[2,768,2,2,64]{1,4,2,3,0:T(8,128)(2,1)S(1)}, s32[8]{0:T(128)S(1)}, s32[2,768]{...) while((s32[]{:T(128)}, ...), condition=%wide.region_4.5_spmd.clone.clone, body=%wide.region_1.4_spmd.clone.clone.sunk | while | flops 625673728 | bytes 12019361 | solution.py:74
  143.9 6.4 %fusion.149 = (f32[2,4,256]{2,1,0:T(4,128)S(1)}, bf16[2,4,256,768]{2,3,1,0:T(8,128)(2,1)}) fusion(s32[2,4]{1,0:T(2,128)S(1)} %lt.125, s32[256,768]{0,1:T(8,128)S(1)} %iota_subtract_fusion.4, pred[256,768]{0,1:T(8,128)(4,1)S(1)} %get-tuple-element.308, pred[256,768]{0,1:T(8,128)(4,1)S(1)} %get-tuple-element.309, ...), kind=kOutput, calls=%fused_computation.100.clone.1 | convolution fusion | flops 423101184 | bytes 6433792 | tf_op jit(solution)/shard_map/while/body/eval_jaxpr/sub | solution.py:68
  150.3 2.5 fusion.150
  153.4 6.4 %fusion.149 = (f32[2,4,256]{2,1,0:T(4,128)S(1)}, bf16[2,4,256,768]{2,3,1,0:T(8,128)(2,1)}) fusion(s32[2,4]{1,0:T(2,128)S(1)} %lt.125, s32[256,768]{0,1:T(8,128)S(1)} %iota_subtract_fusion.4, pred[256,768]{0,1:T(8,128)(4,1)S(1)} %get-tuple-element.308, pred[256,768]{0,1:T(8,128)(4,1)S(1)} %get-tuple-element.309, ...), kind=kOutput, calls=%fused_computation.100.clone.1 | convolution fusion | flops 423101184 | bytes 6433792 | tf_op jit(solution)/shard_map/while/body/eval_jaxpr/sub | solution.py:68
  159.8 2.5 fusion.150
  162.3 0.5 copy.20
  163.0 33.2 %all-gather.11.cloned.1.call-done = bf16[512,2048]{0,1:T(8,128)(2,1)} async-done(((bf16[512,64]{0,1:T(8,128)(2,1)}), bf16[512,2048]{0,1:T(8,128)(2,1)}) %all-gather.11.cloned.1.call-update) | async-done | bytes 2097168 | tf_op jit(solution)/shard_map/all_gather | solution.py:80
  196.2 4.9 fusion.122
  201.2 58.2 %reduce-scatter.3.cloned.1.call-done = f32[512,512]{1,0:T(8,128)} async-done(((f32[512,2048]{1,0:T(8,128)}), f32[512,512]{1,0:T(8,128)}) %reduce-scatter.3.cloned.1.call-update) | async-done | bytes 1048592 | tf_op jit(solution)/shard_map/reduce_scatter | solution.py:82
  259.4 2.2 fusion.110
  262.4 28.5 %all-gather.13.cloned.1.call-done = bf16[512,2048]{1,0:T(8,128)(2,1)} async-done(((bf16[512,512]{1,0:T(8,128)(2,1)}), bf16[512,2048]{1,0:T(8,128)(2,1)}) %all-gather.13.cloned.1.call-update) | async-done | bytes 2097168 | tf_op jit(solution)/shard_map/all_gather | solution.py:107
  291.0 2.1 fusion.98
  293.0 75.1 %all-gather.15.cloned.1.call-done = bf16[2048,768]{1,0:T(8,128)(2,1)} async-done(((bf16[64,768]{1,0:T(8,128)(2,1)}), bf16[2048,768]{1,0:T(8,128)(2,1)}) %all-gather.15.cloned.1.call-update) | async-done | bytes 3145744 | tf_op jit(solution)/shard_map/all_gather | solution.py:35
  368.1 4.4 fusion.107
  373.1 1.3 collective-permute-start.4
  374.5 4.0 collective-permute-done.4
  378.4 3.4 collective-permute-start.5
  381.9 3.2 collective-permute-start.6
  385.1 1.3 collective-permute-start.7
  386.3 1.2 collective-permute-done.7
  387.6 3.1 collective-permute-start.8
  390.6 2.4 collective-permute-start.9
  393.1 2.3 collective-permute-done.8
  396.0 0.8 pad_maximum_fusion.1
  396.9 19.0 %while.25 = (s32[]{:T(128)}, bf16[2,256,2,4,64]{1,4,3,2,0:T(8,128)(2,1)S(1)}, bf16[2,768,2,2,64]{1,4,2,3,0:T(8,128)(2,1)S(1)}, s32[8]{0:T(128)S(1)}, s32[2,768]{...) while((s32[]{:T(128)}, ...), condition=%wide.region_10.11_spmd.clone.clone, body=%wide.region_7.10_spmd.clone.clone.sunk | while | flops 625673728 | bytes 12019361 | solution.py:74
  397.4 6.4 %fusion.155 = (f32[2,4,256]{2,1,0:T(4,128)S(1)}, bf16[2,4,256,768]{2,3,1,0:T(8,128)(2,1)}) fusion(s32[2,4]{1,0:T(2,128)S(1)} %lt.129, s32[256,768]{0,1:T(8,128)S(1)} %iota_subtract_fusion.5, pred[256,768]{0,1:T(8,128)(4,1)S(1)} %get-tuple-element.319, pred[256,768]{0,1:T(8,128)(4,1)S(1)} %get-tuple-element.320, ...), kind=kOutput, calls=%fused_computation.101.clone.1 | convolution fusion | flops 423101184 | bytes 6433792 | tf_op jit(solution)/shard_map/while/body/eval_jaxpr/sub | solution.py:68
  403.8 2.6 fusion.156
  406.9 6.4 %fusion.155 = (f32[2,4,256]{2,1,0:T(4,128)S(1)}, bf16[2,4,256,768]{2,3,1,0:T(8,128)(2,1)}) fusion(s32[2,4]{1,0:T(2,128)S(1)} %lt.129, s32[256,768]{0,1:T(8,128)S(1)} %iota_subtract_fusion.5, pred[256,768]{0,1:T(8,128)(4,1)S(1)} %get-tuple-element.319, pred[256,768]{0,1:T(8,128)(4,1)S(1)} %get-tuple-element.320, ...), kind=kOutput, calls=%fused_computation.101.clone.1 | convolution fusion | flops 423101184 | bytes 6433792 | tf_op jit(solution)/shard_map/while/body/eval_jaxpr/sub | solution.py:68
  413.3 2.5 fusion.156
  416.5 31.9 %all-gather.17.cloned.1.call-done = bf16[512,2048]{0,1:T(8,128)(2,1)} async-done(((bf16[512,64]{0,1:T(8,128)(2,1)}), bf16[512,2048]{0,1:T(8,128)(2,1)}) %all-gather.17.cloned.1.call-update) | async-done | bytes 2097168 | tf_op jit(solution)/shard_map/all_gather | solution.py:80
  448.4 4.9 fusion.123
  453.4 58.3 %reduce-scatter.5.cloned.1.call-done = f32[512,512]{1,0:T(8,128)} async-done(((f32[512,2048]{1,0:T(8,128)}), f32[512,512]{1,0:T(8,128)}) %reduce-scatter.5.cloned.1.call-update) | async-done | bytes 1048592 | tf_op jit(solution)/shard_map/reduce_scatter | solution.py:82
  511.7 2.2 add_convert_fusion
  (73 shorter events, 6.4 us)
Async XLA Ops:
  6.5 36.0 %all-gather.7.cloned.1.call-start = ((), (), s32[]{:S(2)}) async-start(), calls=%async_computation.2 | async-start | bytes 2621440 | tf_op jit(solution)/shard_map/all_gather | solution.py:98
  7.3 112.5 %all-gather.9.cloned.1.call-start = ((), (), s32[]{:S(2)}) async-start(), calls=%async_computation.3 | async-start | bytes 3244032 | tf_op jit(solution)/shard_map/all_gather | solution.py:35
  8.0 188.2 %all-gather.11.cloned.1.call-start = ((), (), s32[]{:S(2)}) async-start(), calls=%async_computation.4 | async-start | bytes 2162688 | tf_op jit(solution)/shard_map/all_gather | solution.py:80
  8.7 250.7 %reduce-scatter.3.cloned.1.call-start = ((), (), s32[]{:S(2)}) async-start(), calls=%async_computation.5 | async-start | bytes 5242880 | tf_op jit(solution)/shard_map/reduce_scatter | solution.py:82
  42.5 2.2 copy-start
  123.5 7.3 %copy-start.3 = (s32[1,2,256]{2,1,0:T(2,128)S(1)}, s32[1,2,256]{2,1,0:T(2,128)}, u32[]{:S(2)}) copy-start(s32[1,2,256]{2,1,0:T(2,128)} %param.13) | copy-start | bytes 6148
  123.5 12.9 %copy-start.4 = (s32[32]{0:T(128)S(1)}, s32[32]{0:T(128)}, u32[]{:S(2)}) copy-start(s32[32]{0:T(128)} %param.14) | copy-start | bytes 388
  124.1 18.3 %collective-permute-start = (bf16[2,256,2,2,64]{1,0,4,3,2:T(2,128)(2,1)S(1)}, bf16[2,256,2,2,64]{1,0,4,3,2:T(2,128)(2,1)S(1)}, u32[]{:S(2)}, u32[]{:S(2)}) collective-permute-start(bf16[2,256,2,2,64]{1,0,4,3,2:T(2,128)(2,1)S(1)} %slice.48), channel_id=1, source_target_pairs={{0,8},{4,12},{8,16},{12,20},{16,24},{20,28},{24,32},{28,36},{32,40... | collective-permute-start | bytes 786440 | tf_op jit(solution)/shard_map/ppermute | solution.py:17
  127.6 14.8 %collective-permute-start.1 = (bf16[2,256,2,2,64]{1,0,4,3,2:T(2,128)(2,1)S(1)}, bf16[2,256,2,2,64]{1,0,4,3,2:T(2,128)(2,1)S(1)}, u32[]{:S(2)}, u32[]{:S(2)}) collective-permute-start(bf16[2,256,2,2,64]{1,0,4,3,2:T(2,128)(2,1)S(1)} %slice.48), channel_id=1, source_target_pairs={{0,4},{4,8},{8,12},{12,16},{16,20},{20,24},{24,28},{28,32},{32,36}... | collective-permute-start | bytes 786440 | tf_op jit(solution)/shard_map/ppermute | solution.py:17
  130.8 11.1 %collective-permute-start.2 = (s32[2,256]{1,0:T(2,128)S(1)}, s32[2,256]{1,0:T(2,128)S(1)}, u32[]{:S(2)}, u32[]{:S(2)}) collective-permute-start(s32[2,256]{1,0:T(2,128)S(1)} %bitcast.216), channel_id=1, source_target_pairs={{0,8},{4,12},{8,16},{12,20},{16,24},{20,28},{24,32},{28,36},{32,40... | collective-permute-start | bytes 6152 | tf_op jit(solution)/shard_map/ppermute | solution.py:17
  133.9 8.1 %collective-permute-start.3 = (s32[2,256]{1,0:T(2,128)S(1)}, s32[2,256]{1,0:T(2,128)S(1)}, u32[]{:S(2)}, u32[]{:S(2)}) collective-permute-start(s32[2,256]{1,0:T(2,128)S(1)} %bitcast.217), channel_id=1, source_target_pairs={{0,4},{4,8},{8,12},{12,16},{16,20},{20,24},{24,28},{28,32},{32,36}... | collective-permute-start | bytes 6152 | tf_op jit(solution)/shard_map/ppermute | solution.py:17
  201.2 58.3 %copy-start.2 = (bf16[1,2,256,512]{3,2,1,0:T(8,128)(2,1)S(1)}, bf16[1,2,256,512]{3,2,1,0:T(8,128)(2,1)}, u32[]{:S(2)}) copy-start(bf16[1,2,256,512]{3,2,1,0:T(8,128)(2,1)} %param.12) | copy-start | bytes 1572868
  201.2 89.8 %all-gather.13.cloned.1.call-start = ((), (), s32[]{:S(2)}) async-start(), calls=%async_computation.6 | async-start | bytes 2621440 | tf_op jit(solution)/shard_map/all_gather | solution.py:107
  261.6 106.5 %all-gather.15.cloned.1.call-start = ((), (), s32[]{:S(2)}) async-start(), calls=%async_computation.7 | async-start | bytes 3244032 | tf_op jit(solution)/shard_map/all_gather | solution.py:35
  262.2 186.2 %all-gather.17.cloned.1.call-start = ((), (), s32[]{:S(2)}) async-start(), calls=%async_computation.8 | async-start | bytes 2162688 | tf_op jit(solution)/shard_map/all_gather | solution.py:80
  373.1 5.3 %collective-permute-start.4 = (bf16[2,256,2,2,64]{1,0,4,3,2:T(2,128)(2,1)S(1)}, bf16[2,256,2,2,64]{1,0,4,3,2:T(2,128)(2,1)S(1)}, u32[]{:S(2)}, u32[]{:S(2)}) collective-permute-start(bf16[2,256,2,2,64]{1,0,4,3,2:T(2,128)(2,1)S(1)} %slice.50), channel_id=1, source_target_pairs={{0,128},{128,0},{1,129},{129,1},{2,130},{130,2},{3,131},{131,3},{4... | collective-permute-start | bytes 786440 | tf_op jit(solution)/shard_map/ppermute | solution.py:23
  374.4 137.2 %reduce-scatter.5.cloned.1.call-start = ((), (), s32[]{:S(2)}) async-start(), calls=%async_computation.9 | async-start | bytes 5242880 | tf_op jit(solution)/shard_map/reduce_scatter | solution.py:82
  378.4 17.5 %collective-permute-start.5 = (bf16[2,256,2,2,64]{1,0,4,3,2:T(2,128)(2,1)S(1)}, bf16[2,256,2,2,64]{1,0,4,3,2:T(2,128)(2,1)S(1)}, u32[]{:S(2)}, u32[]{:S(2)}) collective-permute-start(bf16[2,256,2,2,64]{1,0,4,3,2:T(2,128)(2,1)S(1)} %collective-permute-done.4), channel_id=1, source_target_pairs={{0,8},{4,12},{8,16},{12,20},{16,24},{20,28},{24,32},{28,36},{32,40... | collective-permute-start | bytes 786440 | tf_op jit(solution)/shard_map/ppermute | solution.py:17
  381.9 14.1 %collective-permute-start.6 = (bf16[2,256,2,2,64]{1,0,4,3,2:T(2,128)(2,1)S(1)}, bf16[2,256,2,2,64]{1,0,4,3,2:T(2,128)(2,1)S(1)}, u32[]{:S(2)}, u32[]{:S(2)}) collective-permute-start(bf16[2,256,2,2,64]{1,0,4,3,2:T(2,128)(2,1)S(1)} %collective-permute-done.4), channel_id=1, source_target_pairs={{0,4},{4,8},{8,12},{12,16},{16,20},{20,24},{24,28},{28,32},{32,36}... | collective-permute-start | bytes 786440 | tf_op jit(solution)/shard_map/ppermute | solution.py:17
  385.1 2.5 collective-permute-start.7
  387.6 7.9 %collective-permute-start.8 = (s32[2,256]{1,0:T(2,128)S(1)}, s32[2,256]{1,0:T(2,128)S(1)}, u32[]{:S(2)}, u32[]{:S(2)}) collective-permute-start(s32[2,256]{1,0:T(2,128)S(1)} %collective-permute-done.7), channel_id=1, source_target_pairs={{0,8},{4,12},{8,16},{12,20},{16,24},{20,28},{24,32},{28,36},{32,40... | collective-permute-start | bytes 6152 | tf_op jit(solution)/shard_map/ppermute | solution.py:17
  390.6 4.8 collective-permute-start.9
  453.4 58.3 %copy-start.1 = (bf16[512,512]{1,0:T(8,128)(2,1)S(1)}, bf16[512,512]{1,0:T(8,128)(2,1)}, u32[]{:S(2)}) copy-start(bf16[512,512]{1,0:T(8,128)(2,1)} %fusion.110) | copy-start | bytes 1572868
Sparse Core Ops, SparseCore 0:
  9.1 33.3 all-gather.6
  45.1 74.6 all-gather.8
  122.4 73.7 all-gather.10
  201.3 58.0 reduce-scatter.2
  261.8 29.1 all-gather.12
  293.4 74.6 all-gather.14
  374.5 73.8 all-gather.16
  453.5 58.0 reduce-scatter.4
where the time goes:
time: 521 us
  waiting for transfers between devices  408 us (78%)
  matrix products  53.8 us (10%)
  starting transfers between devices  27.2 us (5%)
  between operations  13.8 us (3%)
  other arithmetic  12.2 us (2%)
    all_gather x2, waiting for transfers between devices, project_in(): lax.all_gather(weight_rows, 'tm', axis=0, tiled=True)  150 us
    reduce_scatter x2, waiting for transfers between devices, project_out(): summed = lax.psum_scatter(terms, 'mp', scatter_dimension=1, tiled=True)  116 us
    all_gather x2, waiting for transfers between devices, project_out(): lax.all_gather(weight, 'tm', axis=1, tiled=True)  65.2 us
    all_gather x1, waiting for transfers between devices, body(): full = lax.all_gather(motion, 'mp', axis=3, tiled=True).reshape(count, D)  32.9 us
    all_gather x1, waiting for transfers between devices, body(): hidden_full = lax.all_gather(hidden, 'mp', axis=1, tiled=True)  28.5 us
    sub x4, matrix products, one_clip(): exps = jnp.where(allowed, jnp.exp(scores - top), 0.0)  25.7 us
    ppermute x8, starting transfers between devices, passed_along(): lax.ppermute(value, axis, [(source, source + steps) for source in range(l...  24.2 us
  transfers between devices with their start and end apart: 18, of which 13 were waited for; matrix products, arithmetic and copies ran while one was open for 10% of the time, Pallas kernels for 0%

commit v1 on v0

--- a/solution.py
+++ b/solution.py
@@ -32,7 +32,9 @@
 def project_in(normed_rows, weight_rows):
     total = jnp.dot(
         normed_rows,
-        lax.all_gather(weight_rows, "tm", axis=0, tiled=True),
+        jnp.concatenate(
+            lax.all_to_all(jnp.stack([weight_rows] * lax.axis_size("tm")), "tm", 0, 0), axis=0
+        ),
         preferred_element_type=jnp.float32,
     )
     return total.astype(jnp.bfloat16)

time: 521 us -> 399 us (0.77)
  waiting for transfers between devices: 408 us -> 252 us
  starting transfers between devices: 27.2 us -> 52.4 us
  local copies, waits for them, and re-layouts: 5.06 us -> 12.4 us
    all_gather x2 -> x0, waiting for transfers between devices: 150 us -> none  [project_in(): lax.all_gather(weight_rows, 'tm', axis=0, tiled=True)]
    all_gather x2, waiting for transfers between devices: 65.2 us -> 24.8 us  [project_out(): lax.all_gather(weight, 'tm', axis=1, tiled=True)]
    all_to_all x0 -> x2, waiting for transfers between devices: none -> 34.9 us  [project_in(): lax.all_to_all(jnp.stack([weight_rows] * lax.axis_size('tm')), 'tm', 0, 0)]
    all_to_all x0 -> x2, starting transfers between devices: none -> 24 us  [project_in(): lax.all_to_all(jnp.stack([weight_rows] * lax.axis_size('tm')), 'tm', 0, 0)]
    reduce_scatter x2, waiting for transfers between devices: 116 us -> 105 us  [project_out(): summed = lax.psum_scatter(terms, 'mp', scatter_dimension=1, tiled=True)]
    ppermute x8, waiting for transfers between devices: 7.96 us -> 15.2 us  [passed_along(): lax.ppermute(value, axis, [(source, source + steps) for source in range(l...]
  transfers between devices with their start and end apart: 18 -> 18, of which waited for: 13 -> 11; matrix products, arithmetic and copies ran while one was open for 10% -> 15% of each run, Pallas kernels for 0% -> 0%
where the time goes in v1:
time: 399 us; the launch traced here: 398 us
  waiting for transfers between devices  252 us (63%)
  matrix products  54 us (14%)
  starting transfers between devices  52.4 us (13%)
  between operations  13.8 us (3%)
  other arithmetic  13.7 us (3%)
  local copies, waits for them, and re-layouts  12.4 us (3%)
    reduce_scatter x2, waiting for transfers between devices, project_out(): summed = lax.psum_scatter(terms, 'mp', scatter_dimension=1, tiled=True)  105 us
    all_to_all x2, waiting for transfers between devices, project_in(): lax.all_to_all(jnp.stack([weight_rows] * lax.axis_size('tm')), 'tm', 0, 0)  34.9 us
    all_gather x1, waiting for transfers between devices, body(): full = lax.all_gather(motion, 'mp', axis=3, tiled=True).reshape(count, D)  32.2 us
    all_gather x1, waiting for transfers between devices, body(): hidden_full = lax.all_gather(hidden, 'mp', axis=1, tiled=True)  29.1 us
    ppermute x8, starting transfers between devices, passed_along(): lax.ppermute(value, axis, [(source, source + steps) for source in range(l...  27.2 us
    sub x4, matrix products, one_clip(): exps = jnp.where(allowed, jnp.exp(scores - top), 0.0)  25.5 us
    all_gather x2, waiting for transfers between devices, project_out(): lax.all_gather(weight, 'tm', axis=1, tiled=True)  24.8 us
    all_to_all x2, starting transfers between devices, project_in(): lax.all_to_all(jnp.stack([weight_rows] * lax.axis_size('tm')), 'tm', 0, 0)  24 us
  transfers between devices with their start and end apart: 18, of which 11 were waited for; matrix products, arithmetic and copies ran while one was open for 15% of the time, Pallas kernels for 0%

profile of v1, /device:TPU:1, one launch (start us, length us, event | category | flops | bytes accessed | tf_op | source)
XLA Modules:
  0.0 398.5 jit_solution(5729890521415931133)
XLA Ops:
  6.5 2.9 stack.4
  9.4 12.2 %all-to-all-start = ((bf16[32,64,768]{2,1,0:T(8,128)(2,1)}), bf16[32,64,768]{2,1,0:T(8,128)(2,1)S(1)}, u32[]{:S(2)}, u32[]{:S(2)}) async-start(bf16[32,64,768]{2,1,0:T(8,128)(2,1)} %stack.4), calls=%async_computation | async-start | bytes 6291456 | tf_op jit(solution)/shard_map/all_to_all | solution.py:36
  21.6 0.7 all-gather.5.cloned.1.call-update
  22.4 0.7 all-gather.7.cloned.1.call-update
  23.2 32.2 %all-gather.5.cloned.1.call-done = bf16[1,2,256,2048]{3,2,1,0:T(8,128)(2,1)} async-done(((bf16[1,2,256,512]{3,2,1,0:T(8,128)(2,1)}), bf16[1,2,256,2048]{3,2,1,0:T(8,128)(2,1)}) %all-gather.5.cloned.1.call-update) | async-done | bytes 2097168 | tf_op jit(solution)/shard_map/all_gather | solution.py:100
  55.3 2.2 fusion.98
  57.6 1.9 fusion.100
  59.5 34.9 %all-to-all-done = bf16[32,64,768]{2,1,0:T(8,128)(2,1)S(1)} async-done(((bf16[32,64,768]{2,1,0:T(8,128)(2,1)}), bf16[32,64,768]{2,1,0:T(8,128)(2,1)S(1)}, u32[]{:S(2)}, u32[]{:S(2)}) %all-to-all-start) | async-done | bytes 3145760 | tf_op jit(solution)/shard_map/all_to_all | solution.py:36
  94.4 4.3 %convolution_convert_fusion = bf16[512,768]{1,0:T(8,128)(2,1)} fusion(bf16[512,2048]{1,0:T(8,128)(2,1)} %bitcast.209, bf16[2048,768]{1,0:T(8,128)(2,1)S(1)} %bitcast.205), kind=kOutput, calls=%fused_computation.89 | convolution fusion | flops 1611005952 | bytes 6029312 | tf_op jit(solution)/shard_map/dot_general | solution.py:33
  98.7 1.4 copy.17
  100.5 4.9 %collective-permute-start = (bf16[2,256,2,2,64]{1,0,4,3,2:T(2,128)(2,1)S(1)}, bf16[2,256,2,2,64]{1,0,4,3,2:T(2,128)(2,1)S(1)}, u32[]{:S(2)}, u32[]{:S(2)}) collective-permute-start(bf16[2,256,2,2,64]{1,0,4,3,2:T(2,128)(2,1)S(1)} %slice.48), channel_id=1, source_target_pairs={{0,8},{4,12},{8,16},{12,20},{16,24},{20,28},{24,32},{28,36},{32,40... | collective-permute-start | bytes 786440 | tf_op jit(solution)/shard_map/ppermute | solution.py:17
  105.4 4.5 %collective-permute-start.1 = (bf16[2,256,2,2,64]{1,0,4,3,2:T(2,128)(2,1)S(1)}, bf16[2,256,2,2,64]{1,0,4,3,2:T(2,128)(2,1)S(1)}, u32[]{:S(2)}, u32[]{:S(2)}) collective-permute-start(bf16[2,256,2,2,64]{1,0,4,3,2:T(2,128)(2,1)S(1)} %slice.48), channel_id=1, source_target_pairs={{0,4},{4,8},{8,12},{12,16},{16,20},{20,24},{24,28},{28,32},{32,36}... | collective-permute-start | bytes 786440 | tf_op jit(solution)/shard_map/ppermute | solution.py:17
  109.8 1.9 collective-permute-start.2
  111.7 1.9 collective-permute-start.3
  113.8 10.7 %collective-permute-done.2 = s32[2,256]{1,0:T(2,128)S(1)} collective-permute-done((s32[2,256]{1,0:T(2,128)S(1)}, s32[2,256]{1,0:T(2,128)S(1)}, u32[]{:S(2)}, u32[]{:S(2)}) %collective-permute-start.2) | collective-permute-done | bytes 2080 | tf_op jit(solution)/shard_map/ppermute | solution.py:17
  125.0 0.8 pad_maximum_fusion
  125.9 18.9 %while.24 = (s32[]{:T(128)}, bf16[2,256,2,4,64]{1,4,3,2,0:T(8,128)(2,1)S(1)}, bf16[2,768,2,2,64]{1,4,2,3,0:T(8,128)(2,1)S(1)}, s32[8]{0:T(128)S(1)}, s32[2,768]{...) while((s32[]{:T(128)}, ...), condition=%wide.region_4.5_spmd.clone.clone, body=%wide.region_1.4_spmd.clone.clone.sunk | while | flops 625673728 | bytes 12019361 | solution.py:76
  126.4 6.4 %fusion.150 = (f32[2,4,256]{2,1,0:T(4,128)S(1)}, bf16[2,4,256,768]{2,3,1,0:T(8,128)(2,1)}) fusion(s32[2,4]{1,0:T(2,128)S(1)} %lt.125, s32[256,768]{0,1:T(8,128)S(1)} %iota_subtract_fusion.4, pred[256,768]{0,1:T(8,128)(4,1)S(1)} %get-tuple-element.308, pred[256,768]{0,1:T(8,128)(4,1)S(1)} %get-tuple-element.309, ...), kind=kOutput, calls=%fused_computation.101.clone.1 | convolution fusion | flops 423101184 | bytes 6433792 | tf_op jit(solution)/shard_map/while/body/eval_jaxpr/sub | solution.py:70
  132.8 2.6 fusion.151
  135.9 6.4 %fusion.150 = (f32[2,4,256]{2,1,0:T(4,128)S(1)}, bf16[2,4,256,768]{2,3,1,0:T(8,128)(2,1)}) fusion(s32[2,4]{1,0:T(2,128)S(1)} %lt.125, s32[256,768]{0,1:T(8,128)S(1)} %iota_subtract_fusion.4, pred[256,768]{0,1:T(8,128)(4,1)S(1)} %get-tuple-element.308, pred[256,768]{0,1:T(8,128)(4,1)S(1)} %get-tuple-element.309, ...), kind=kOutput, calls=%fused_computation.101.clone.1 | convolution fusion | flops 423101184 | bytes 6433792 | tf_op jit(solution)/shard_map/while/body/eval_jaxpr/sub | solution.py:70
  142.2 2.5 fusion.151
  145.5 4.9 %fusion.123 = f32[512,2048]{1,0:T(8,128)} fusion(bf16[512,512]{0,1:T(8,128)(2,1)S(1)} %bitcast.203, bf16[512,2048]{0,1:T(8,128)(2,1)} %all-gather.7.cloned.1.call-done), kind=kOutput, calls=%fused_computation.104 | convolution fusion | flops 1073741824 | bytes 6815744 | tf_op jit(solution)/shard_map/dot_general | solution.py:81
  150.3 0.9 copy-done.2
  151.2 2.0 stack.5
  153.2 11.9 %all-to-all-start.1 = ((bf16[32,64,768]{2,1,0:T(8,128)(2,1)}), bf16[32,64,768]{2,1,0:T(8,128)(2,1)S(1)}, u32[]{:S(2)}, u32[]{:S(2)}) async-start(bf16[32,64,768]{2,1,0:T(8,128)(2,1)} %stack.5), calls=%async_computation.2 | async-start | bytes 6291456 | tf_op jit(solution)/shard_map/all_to_all | solution.py:36
  165.2 46.4 %reduce-scatter.3.cloned.1.call-done = f32[512,512]{1,0:T(8,128)} async-done(((f32[512,2048]{1,0:T(8,128)}), f32[512,512]{1,0:T(8,128)}) %reduce-scatter.3.cloned.1.call-update) | async-done | bytes 1048592 | tf_op jit(solution)/shard_map/reduce_scatter | solution.py:84
  211.6 2.3 fusion.111
  214.1 29.1 %all-gather.9.cloned.1.call-done = bf16[512,2048]{1,0:T(8,128)(2,1)} async-done(((bf16[512,512]{1,0:T(8,128)(2,1)}), bf16[512,2048]{1,0:T(8,128)(2,1)}) %all-gather.9.cloned.1.call-update) | async-done | bytes 2097168 | tf_op jit(solution)/shard_map/all_gather | solution.py:109
  243.2 2.1 fusion.101
  245.3 4.3 %fusion.108 = bf16[512,768]{1,0:T(8,128)(2,1)} fusion(bf16[2048,768]{1,0:T(8,128)(2,1)S(1)} %bitcast.206, bf16[512,2048]{1,0:T(8,128)(2,1)} %all-gather.9.cloned.1.call-done, f32[2048]{0:T(1024)S(1)} %bitcast.211, f32[512]{0:T(512)S(1)} %add_rsqrt_fusion), kind=kOutput, calls=%fused_computation.90 | convolution fusion | flops 1615200256 | bytes 6039552 | tf_op jit(solution)/shard_map/dot_general | solution.py:33
  249.7 1.4 copy.21
  251.9 7.2 %collective-permute-done.4 = bf16[2,256,2,2,64]{1,0,4,3,2:T(2,128)(2,1)S(1)} collective-permute-done((bf16[2,256,2,2,64]{1,0,4,3,2:T(2,128)(2,1)S(1)}, bf16[2,256,2,2,64]{1,0,4,3,2:T(2,128)(2,1)S(1)}, u32[]{:S(2)}, u32[]{:S(2)}) %collective-permute-start.4) | collective-permute-done | bytes 262176 | tf_op jit(solution)/shard_map/ppermute | solution.py:23
  259.1 4.2 %collective-permute-start.5 = (bf16[2,256,2,2,64]{1,0,4,3,2:T(2,128)(2,1)S(1)}, bf16[2,256,2,2,64]{1,0,4,3,2:T(2,128)(2,1)S(1)}, u32[]{:S(2)}, u32[]{:S(2)}) collective-permute-start(bf16[2,256,2,2,64]{1,0,4,3,2:T(2,128)(2,1)S(1)} %collective-permute-done.4), channel_id=1, source_target_pairs={{0,8},{4,12},{8,16},{12,20},{16,24},{20,28},{24,32},{28,36},{32,40... | collective-permute-start | bytes 786440 | tf_op jit(solution)/shard_map/ppermute | solution.py:17
  263.3 3.2 collective-permute-start.6
  266.9 2.5 collective-permute-done.7
  269.4 4.4 %collective-permute-start.8 = (s32[2,256]{1,0:T(2,128)S(1)}, s32[2,256]{1,0:T(2,128)S(1)}, u32[]{:S(2)}, u32[]{:S(2)}) collective-permute-start(s32[2,256]{1,0:T(2,128)S(1)} %collective-permute-done.7), channel_id=1, source_target_pairs={{0,8},{4,12},{8,16},{12,20},{16,24},{20,28},{24,32},{28,36},{32,40... | collective-permute-start | bytes 6152 | tf_op jit(solution)/shard_map/ppermute | solution.py:17
  273.9 2.3 collective-permute-start.9
  276.2 4.4 %collective-permute-done.8 = s32[2,256]{1,0:T(2,128)S(1)} collective-permute-done((s32[2,256]{1,0:T(2,128)S(1)}, s32[2,256]{1,0:T(2,128)S(1)}, u32[]{:S(2)}, u32[]{:S(2)}) %collective-permute-start.8) | collective-permute-done | bytes 2080 | tf_op jit(solution)/shard_map/ppermute | solution.py:17
  281.1 0.8 pad_maximum_fusion.1
  282.0 18.9 %while.25 = (s32[]{:T(128)}, bf16[2,256,2,4,64]{1,4,3,2,0:T(8,128)(2,1)S(1)}, bf16[2,768,2,2,64]{1,4,2,3,0:T(8,128)(2,1)S(1)}, s32[8]{0:T(128)S(1)}, s32[2,768]{...) while((s32[]{:T(128)}, ...), condition=%wide.region_10.11_spmd.clone.clone, body=%wide.region_7.10_spmd.clone.clone.sunk | while | flops 625673728 | bytes 12019361 | solution.py:76
  282.5 6.4 %fusion.156 = (f32[2,4,256]{2,1,0:T(4,128)S(1)}, bf16[2,4,256,768]{2,3,1,0:T(8,128)(2,1)}) fusion(s32[2,4]{1,0:T(2,128)S(1)} %lt.129, s32[256,768]{0,1:T(8,128)S(1)} %iota_subtract_fusion.5, pred[256,768]{0,1:T(8,128)(4,1)S(1)} %get-tuple-element.319, pred[256,768]{0,1:T(8,128)(4,1)S(1)} %get-tuple-element.320, ...), kind=kOutput, calls=%fused_computation.102.clone.1 | convolution fusion | flops 423101184 | bytes 6433792 | tf_op jit(solution)/shard_map/while/body/eval_jaxpr/sub | solution.py:70
  288.9 2.5 fusion.157
  291.9 6.4 %fusion.156 = (f32[2,4,256]{2,1,0:T(4,128)S(1)}, bf16[2,4,256,768]{2,3,1,0:T(8,128)(2,1)}) fusion(s32[2,4]{1,0:T(2,128)S(1)} %lt.129, s32[256,768]{0,1:T(8,128)S(1)} %iota_subtract_fusion.5, pred[256,768]{0,1:T(8,128)(4,1)S(1)} %get-tuple-element.319, pred[256,768]{0,1:T(8,128)(4,1)S(1)} %get-tuple-element.320, ...), kind=kOutput, calls=%fused_computation.102.clone.1 | convolution fusion | flops 423101184 | bytes 6433792 | tf_op jit(solution)/shard_map/while/body/eval_jaxpr/sub | solution.py:70
  298.3 2.5 fusion.157
  301.5 24.8 %all-gather.11.cloned.1.call-done = bf16[512,2048]{0,1:T(8,128)(2,1)} async-done(((bf16[512,64]{0,1:T(8,128)(2,1)}), bf16[512,2048]{0,1:T(8,128)(2,1)}) %all-gather.11.cloned.1.call-update) | async-done | bytes 2097168 | tf_op jit(solution)/shard_map/all_gather | solution.py:82
  326.3 4.9 %fusion.124 = f32[512,2048]{1,0:T(8,128)} fusion(bf16[512,512]{0,1:T(8,128)(2,1)S(1)} %bitcast.204, bf16[512,2048]{0,1:T(8,128)(2,1)} %all-gather.11.cloned.1.call-done), kind=kOutput, calls=%fused_computation.105 | convolution fusion | flops 1073741824 | bytes 6815744 | tf_op jit(solution)/shard_map/dot_general | solution.py:81
  331.2 58.3 %reduce-scatter.5.cloned.1.call-done = f32[512,512]{1,0:T(8,128)} async-done(((f32[512,2048]{1,0:T(8,128)}), f32[512,512]{1,0:T(8,128)}) %reduce-scatter.5.cloned.1.call-update) | async-done | bytes 1048592 | tf_op jit(solution)/shard_map/reduce_scatter | solution.py:84
  389.4 2.2 add_convert_fusion
  (74 shorter events, 6.5 us)
Async XLA Ops:
  9.4 13.7 %copy-start.3 = (f32[2,2048]{1,0:T(2,128)S(1)}, f32[2,2048]{1,0:T(2,128)}, u32[]{:S(2)}) copy-start(f32[2,2048]{1,0:T(2,128)} %param.15) | copy-start | bytes 49156
  9.4 84.9 %all-to-all-start = ((bf16[32,64,768]{2,1,0:T(8,128)(2,1)}), bf16[32,64,768]{2,1,0:T(8,128)(2,1)S(1)}, u32[]{:S(2)}, u32[]{:S(2)}) async-start(bf16[32,64,768]{2,1,0:T(8,128)(2,1)} %stack.4), calls=%async_computation | async-start | bytes 6291456 | tf_op jit(solution)/shard_map/all_to_all | solution.py:36
  21.6 33.7 %all-gather.5.cloned.1.call-start = ((), (), s32[]{:S(2)}) async-start(), calls=%async_computation.4 | async-start | bytes 2621440 | tf_op jit(solution)/shard_map/all_gather | solution.py:100
  22.3 123.1 %all-gather.7.cloned.1.call-start = ((), (), s32[]{:S(2)}) async-start(), calls=%async_computation.5 | async-start | bytes 2162688 | tf_op jit(solution)/shard_map/all_gather | solution.py:82
  23.1 188.5 %reduce-scatter.3.cloned.1.call-start = ((), (), s32[]{:S(2)}) async-start(), calls=%async_computation.6 | async-start | bytes 5242880 | tf_op jit(solution)/shard_map/reduce_scatter | solution.py:84
  55.3 2.2 copy-start
  98.7 11.2 %copy-start.4 = (s32[1,2,256]{2,1,0:T(2,128)S(1)}, s32[1,2,256]{2,1,0:T(2,128)}, u32[]{:S(2)}) copy-start(s32[1,2,256]{2,1,0:T(2,128)} %param.13) | copy-start | bytes 6148
  98.7 15.0 %copy-start.5 = (s32[32]{0:T(128)S(1)}, s32[32]{0:T(128)}, u32[]{:S(2)}) copy-start(s32[32]{0:T(128)} %param.14) | copy-start | bytes 388
  100.5 24.5 %collective-permute-start = (bf16[2,256,2,2,64]{1,0,4,3,2:T(2,128)(2,1)S(1)}, bf16[2,256,2,2,64]{1,0,4,3,2:T(2,128)(2,1)S(1)}, u32[]{:S(2)}, u32[]{:S(2)}) collective-permute-start(bf16[2,256,2,2,64]{1,0,4,3,2:T(2,128)(2,1)S(1)} %slice.48), channel_id=1, source_target_pairs={{0,8},{4,12},{8,16},{12,20},{16,24},{20,28},{24,32},{28,36},{32,40... | collective-permute-start | bytes 786440 | tf_op jit(solution)/shard_map/ppermute | solution.py:17
  105.4 19.6 %collective-permute-start.1 = (bf16[2,256,2,2,64]{1,0,4,3,2:T(2,128)(2,1)S(1)}, bf16[2,256,2,2,64]{1,0,4,3,2:T(2,128)(2,1)S(1)}, u32[]{:S(2)}, u32[]{:S(2)}) collective-permute-start(bf16[2,256,2,2,64]{1,0,4,3,2:T(2,128)(2,1)S(1)} %slice.48), channel_id=1, source_target_pairs={{0,4},{4,8},{8,12},{12,16},{16,20},{20,24},{24,28},{28,32},{32,36}... | collective-permute-start | bytes 786440 | tf_op jit(solution)/shard_map/ppermute | solution.py:17
  109.8 14.6 %collective-permute-start.2 = (s32[2,256]{1,0:T(2,128)S(1)}, s32[2,256]{1,0:T(2,128)S(1)}, u32[]{:S(2)}, u32[]{:S(2)}) collective-permute-start(s32[2,256]{1,0:T(2,128)S(1)} %bitcast.212), channel_id=1, source_target_pairs={{0,8},{4,12},{8,16},{12,20},{16,24},{20,28},{24,32},{28,36},{32,40... | collective-permute-start | bytes 6152 | tf_op jit(solution)/shard_map/ppermute | solution.py:17
  111.7 12.8 %collective-permute-start.3 = (s32[2,256]{1,0:T(2,128)S(1)}, s32[2,256]{1,0:T(2,128)S(1)}, u32[]{:S(2)}, u32[]{:S(2)}) collective-permute-start(s32[2,256]{1,0:T(2,128)S(1)} %bitcast.213), channel_id=1, source_target_pairs={{0,4},{4,8},{8,12},{12,16},{16,20},{20,24},{24,28},{28,32},{32,36}... | collective-permute-start | bytes 6152 | tf_op jit(solution)/shard_map/ppermute | solution.py:17
  150.3 0.9 copy-start.2
  153.2 92.1 %all-to-all-start.1 = ((bf16[32,64,768]{2,1,0:T(8,128)(2,1)}), bf16[32,64,768]{2,1,0:T(8,128)(2,1)S(1)}, u32[]{:S(2)}, u32[]{:S(2)}) async-start(bf16[32,64,768]{2,1,0:T(8,128)(2,1)} %stack.5), calls=%async_computation.2 | async-start | bytes 6291456 | tf_op jit(solution)/shard_map/all_to_all | solution.py:36
  165.1 78.1 %all-gather.9.cloned.1.call-start = ((), (), s32[]{:S(2)}) async-start(), calls=%async_computation.7 | async-start | bytes 2621440 | tf_op jit(solution)/shard_map/all_gather | solution.py:109
  213.9 112.4 %all-gather.11.cloned.1.call-start = ((), (), s32[]{:S(2)}) async-start(), calls=%async_computation.8 | async-start | bytes 2162688 | tf_op jit(solution)/shard_map/all_gather | solution.py:82
  251.4 7.7 %collective-permute-start.4 = (bf16[2,256,2,2,64]{1,0,4,3,2:T(2,128)(2,1)S(1)}, bf16[2,256,2,2,64]{1,0,4,3,2:T(2,128)(2,1)S(1)}, u32[]{:S(2)}, u32[]{:S(2)}) collective-permute-start(bf16[2,256,2,2,64]{1,0,4,3,2:T(2,128)(2,1)S(1)} %slice.50), channel_id=1, source_target_pairs={{0,128},{128,0},{1,129},{129,1},{2,130},{130,2},{3,131},{131,3},{4... | collective-permute-start | bytes 786440 | tf_op jit(solution)/shard_map/ppermute | solution.py:23
  251.8 137.6 %reduce-scatter.5.cloned.1.call-start = ((), (), s32[]{:S(2)}) async-start(), calls=%async_computation.9 | async-start | bytes 5242880 | tf_op jit(solution)/shard_map/reduce_scatter | solution.py:84
  259.1 21.9 %collective-permute-start.5 = (bf16[2,256,2,2,64]{1,0,4,3,2:T(2,128)(2,1)S(1)}, bf16[2,256,2,2,64]{1,0,4,3,2:T(2,128)(2,1)S(1)}, u32[]{:S(2)}, u32[]{:S(2)}) collective-permute-start(bf16[2,256,2,2,64]{1,0,4,3,2:T(2,128)(2,1)S(1)} %collective-permute-done.4), channel_id=1, source_target_pairs={{0,8},{4,12},{8,16},{12,20},{16,24},{20,28},{24,32},{28,36},{32,40... | collective-permute-start | bytes 786440 | tf_op jit(solution)/shard_map/ppermute | solution.py:17
  263.3 17.8 %collective-permute-start.6 = (bf16[2,256,2,2,64]{1,0,4,3,2:T(2,128)(2,1)S(1)}, bf16[2,256,2,2,64]{1,0,4,3,2:T(2,128)(2,1)S(1)}, u32[]{:S(2)}, u32[]{:S(2)}) collective-permute-start(bf16[2,256,2,2,64]{1,0,4,3,2:T(2,128)(2,1)S(1)} %collective-permute-done.4), channel_id=1, source_target_pairs={{0,4},{4,8},{8,12},{12,16},{16,20},{20,24},{24,28},{28,32},{32,36}... | collective-permute-start | bytes 786440 | tf_op jit(solution)/shard_map/ppermute | solution.py:17
  266.5 2.9 collective-permute-start.7
  269.4 11.1 %collective-permute-start.8 = (s32[2,256]{1,0:T(2,128)S(1)}, s32[2,256]{1,0:T(2,128)S(1)}, u32[]{:S(2)}, u32[]{:S(2)}) collective-permute-start(s32[2,256]{1,0:T(2,128)S(1)} %collective-permute-done.7), channel_id=1, source_target_pairs={{0,8},{4,12},{8,16},{12,20},{16,24},{20,28},{24,32},{28,36},{32,40... | collective-permute-start | bytes 6152 | tf_op jit(solution)/shard_map/ppermute | solution.py:17
  273.9 6.7 %collective-permute-start.9 = (s32[2,256]{1,0:T(2,128)S(1)}, s32[2,256]{1,0:T(2,128)S(1)}, u32[]{:S(2)}, u32[]{:S(2)}) collective-permute-start(s32[2,256]{1,0:T(2,128)S(1)} %collective-permute-done.7), channel_id=1, source_target_pairs={{0,4},{4,8},{8,12},{12,16},{16,20},{20,24},{24,28},{28,32},{32,36}... | collective-permute-start | bytes 6152 | tf_op jit(solution)/shard_map/ppermute | solution.py:17
  331.2 58.3 %copy-start.1 = (bf16[512,512]{1,0:T(8,128)(2,1)S(1)}, bf16[512,512]{1,0:T(8,128)(2,1)}, u32[]{:S(2)}) copy-start(bf16[512,512]{1,0:T(8,128)(2,1)} %fusion.111) | copy-start | bytes 1572868
Sparse Core Ops, SparseCore 0:
  24.2 31.0 all-gather.4
  57.9 79.5 all-gather.6
  150.5 61.0 reduce-scatter.2
  214.0 29.1 all-gather.8
  252.0 74.2 all-gather.10
  331.3 58.0 reduce-scatter.4
